TPU v7x, 512 devices: a whole 4x8x8 slice. The times are simulated.
512 devices in a mesh: blk: 64 (over x, z, y_lo), rep: 8 (over y_hi, core).
Axes of the slice: x: 4, y: 8 (y_hi: 4, y_lo: 2; y = y_hi * 2 + y_lo), z: 8, core: 2. Of those that a mesh axis runs over, the one named last changes fastest.
Arguments:
- grad_out: bfloat16 [65536, 256], P(('blk', 'rep')), may hold values from -6 to 6
- preact: bfloat16 [65536, 256], P(('blk', 'rep')), may hold values from -6 to 6
- aggregated: bfloat16 [65536, 256], P(('blk', 'rep')), may hold values from -6 to 6
- weight: bfloat16 [256, 256], replicated, may hold values from -0.375 to 0.375
- degree: int32 [65536], P(('blk', 'rep')), may hold values from 4 to 64
- neighbors: int32 [64, 8, 64, 4, 8, 128], P('blk', 'rep'), may hold values from 0 to 127
- tile_col: int32 [64, 8, 64, 4], P('blk', 'rep'), may hold values from 0 to 7, as said below
- tile_count: int32 [64, 8, 64], P('blk', 'rep'), may hold values from 0 to 4, as said below
Outputs:
- grad_features: bfloat16 [65536, 256], P(('blk', 'rep'))
- grad_weight: float32 [256, 256], replicated
Inputs may be any that keep to these rules, and one draw needn't show every extreme that they name: `tile_col`: the column tiles listed for one block, replica and source block are all different, also in slots at or past the count. `tile_count`: equal to 4 wherever the source block equals the block, and 0 wherever the source block is more than 2 blocks away from the block in both directions around the closed loop of 64 blocks.
All inputs are finite; a program needn't handle non-finite values.
Results may differ from a plain program's by a relative error of at most 0.0049.
Values may be sent and summed in bfloat16 or wider, within the bound.
No kernel may reach another device: no remote copies, remote signals or barrier semaphores. Data moves between devices by JAX's collectives and lax.ppermute only.
A program may use at most 64 MiB of HBM per device.

v0:
```python
import jax
import jax.numpy as jnp
from jax import lax
from jax.sharding import PartitionSpec as P

REACH = 2


def fetched_from(x, axis, offset):
    size = lax.axis_size(axis)
    return lax.ppermute(x, axis, [(i, (i - offset) % size) for i in range(size)])


def on_device(grad_out, preact, aggregated, weight, degree, neighbors, tile_col, tile_count):
    grad_pre = jnp.where(preact > 0, grad_out, jnp.zeros_like(grad_out))
    local_weight = lax.dot_general(
        aggregated, grad_pre, (((0,), (0,)), ((), ())), preferred_element_type=jnp.float32
    )
    raw_weight = lax.psum(local_weight, ("blk", "rep"))
    norm_value = jnp.sqrt(jnp.sum(raw_weight * raw_weight) + 1e-06)
    grad_weight = raw_weight * jnp.minimum(1.0, 128.0 / norm_value)
    inv_root = 1.0 / jnp.sqrt(degree.astype(jnp.float32))
    backward = lax.dot_general(
        grad_pre, weight, (((1,), (1,)), ((), ())), preferred_element_type=jnp.float32
    )
    scaled = (backward * inv_root[:, None]).astype(jnp.bfloat16)
    blocks = lax.axis_size("blk")
    replicas = lax.axis_size("rep")
    own_block = lax.axis_index("blk")
    offsets = list(range(-REACH, REACH + 1))
    rows = jnp.stack([scaled if d == 0 else fetched_from(scaled, "blk", d) for d in offsets])
    sources = (own_block + jnp.array(offsets, jnp.int32)) % blocks
    listed = jnp.take(neighbors[0, 0], sources, axis=0)
    column_ids = jnp.take(tile_col[0, 0], sources, axis=0)
    present = jnp.take(tile_count[0, 0], sources, axis=0)
    slots_total = listed.shape[1]
    tile_side = listed.shape[3]
    hidden = scaled.shape[1]
    positions = jnp.arange(tile_side, dtype=jnp.int32)
    slot_index = jnp.arange(slots_total, dtype=jnp.int32)
    counts = jnp.sum(
        (listed[:, :, :, :, None] == positions[None, None, None, None, :]).astype(jnp.int32), axis=2
    )
    chooser = jnp.logical_and(
        column_ids[:, :, None] == jnp.arange(replicas, dtype=jnp.int32)[None, None, :],
        (slot_index[None, :] < present[:, None])[:, :, None],
    ).astype(jnp.int32)
    merged = jnp.einsum("tsn,tsic->tinc", chooser, counts).astype(jnp.bfloat16)
    totals = jnp.einsum("tinc,tif->ncf", merged, rows, preferred_element_type=jnp.float32)
    owned = lax.psum_scatter(totals, "rep", scatter_dimension=0, tiled=True)
    grad_features = (owned[0] * inv_root[:, None]).astype(jnp.bfloat16)
    return (grad_features, grad_weight)


def solution(mesh):
    return jax.shard_map(
        on_device,
        mesh=mesh,
        in_specs=(
            P(("blk", "rep"), None),
            P(("blk", "rep"), None),
            P(("blk", "rep"), None),
            P(),
            P(("blk", "rep")),
            P("blk", "rep", None, None, None, None),
            P("blk", "rep", None, None),
            P("blk", "rep", None),
        ),
        out_specs=(P(("blk", "rep"), None), P()),
        check_vma=False,
    )
```

profile of v0, /device:TPU:23, one launch (start us, length us, event | category | flops | bytes accessed | tf_op | source)
XLA Modules:
  0.0 314.2 jit_solution(9490777069166894730)
XLA Ops:
  8.0 0.0 copy-start
  8.0 0.0 all-reduce.2.cloned.1.call-start
  8.1 0.7 convert_rsqrt_fusion
  8.8 1.2 fusion.2
  10.0 0.0 copy-start.2
  10.0 0.0 copy-start.1
  10.0 4.1 %collective-permute-start = (bf16[128,256]{1,0:T(8,128)(2,1)S(1)}, bf16[128,256]{1,0:T(8,128)(2,1)S(1)}, u32[]{:S(2)}, u32[]{:S(2)}) collective-permute-start(bf16[128,256]{1,0:T(8,128)(2,1)S(1)} %fusion.2), channel_id=1, source_target_pairs={{0,16},{8,24},{16,32},{24,40},{32,48},{40,56},{48,64},{56,72},{64,... | collective-permute-start | bytes 196616 | tf_op jit(solution)/shard_map/ppermute | solution.py:11
  14.1 3.2 %collective-permute-start.1 = (bf16[128,256]{1,0:T(8,128)(2,1)S(1)}, bf16[128,256]{1,0:T(8,128)(2,1)S(1)}, u32[]{:S(2)}, u32[]{:S(2)}) collective-permute-start(bf16[128,256]{1,0:T(8,128)(2,1)S(1)} %fusion.2), channel_id=1, source_target_pairs={{0,8},{8,16},{16,24},{24,32},{32,40},{40,48},{48,56},{56,64},{64,7... | collective-permute-start | bytes 196616 | tf_op jit(solution)/shard_map/ppermute | solution.py:11
  17.4 8.6 %collective-permute-start.2 = (bf16[128,256]{1,0:T(8,128)(2,1)S(1)}, bf16[128,256]{1,0:T(8,128)(2,1)S(1)}, u32[]{:S(2)}, u32[]{:S(2)}) collective-permute-start(bf16[128,256]{1,0:T(8,128)(2,1)S(1)} %fusion.2), channel_id=1, source_target_pairs={{0,504},{8,0},{16,8},{24,16},{32,24},{40,32},{48,40},{56,48},{64,5... | collective-permute-start | bytes 196616 | tf_op jit(solution)/shard_map/ppermute | solution.py:11
  25.9 3.4 %collective-permute-start.3 = (bf16[128,256]{1,0:T(8,128)(2,1)S(1)}, bf16[128,256]{1,0:T(8,128)(2,1)S(1)}, u32[]{:S(2)}, u32[]{:S(2)}) collective-permute-start(bf16[128,256]{1,0:T(8,128)(2,1)S(1)} %fusion.2), channel_id=1, source_target_pairs={{0,496},{8,504},{16,0},{24,8},{32,16},{40,24},{48,32},{56,40},{64,... | collective-permute-start | bytes 196616 | tf_op jit(solution)/shard_map/ppermute | solution.py:11
  29.3 1.8 convolution_bitcast_fusion.2
  31.1 0.0 all-reduce.2.cloned.1.call-update
  31.2 0.0 reduce-scatter.2.cloned.1.call-start
  31.2 0.7 compare_and_fusion
  31.9 0.0 copy-done
  31.9 0.6 gather_fusion
  32.5 0.1 broadcast_select_fusion
  32.5 4.2 %convert_reduce_fusion = s32[5,4,128,128]{3,2,1,0:T(8,128)S(1)} fusion(s32[5,4,8,128]{3,2,1,0:T(8,128)S(1)} %broadcast_select_fusion), kind=kLoop, calls=%fused_computation.3 | loop fusion | flops 7536640 | bytes 1392640 | tf_op jit(solution)/shard_map/reduce_sum | solution.py:41
  36.7 0.0 copy-done.2
  36.7 0.1 copy.15
  36.8 0.6 gather_fusion.1
  37.4 0.1 broadcast_select_fusion.1
  37.4 0.0 copy-done.1
  37.4 0.6 gather_fusion.2
  38.1 0.1 iota_compare_fusion.2
  38.2 2.8 convolution_bitcast_fusion
  41.0 0.0 collective-permute-done
  41.0 0.0 collective-permute-done.1
  41.1 0.0 collective-permute-done.2
  41.1 0.0 collective-permute-done.3
  41.1 1.6 convolution_bitcast_fusion.1
  42.7 0.0 reduce-scatter.2.cloned.1.call-update
  42.7 258.3 %all-reduce.2.cloned.1.call-done = f32[256,256]{0,1:T(8,128)} async-done(((f32[256,256]{0,1:T(8,128)}), f32[256,256]{0,1:T(8,128)}) %all-reduce.2.cloned.1.call-update) | async-done | bytes 262160 | tf_op jit(solution)/shard_map/psum | solution.py:19
  301.0 1.6 multiply_reduce_fusion
  303.3 1.0 broadcast_multiply_fusion
  304.3 0.8 copy.18
  305.2 0.0 reduce-scatter.2.cloned.1.call-done
  305.2 1.6 fusion.4
  (7 shorter events, 0.0 us)
Async XLA Ops:
  8.0 23.9 %copy-start = (s32[1,1,64,4,8,128]{5,4,3,2,1,0:T(8,128)S(1)}, s32[1,1,64,4,8,128]{5,4,3,2,1,0:T(8,128)}, u32[]{:S(2)}) copy-start(s32[1,1,64,4,8,128]{5,4,3,2,1,0:T(8,128)} %param.14) | copy-start | bytes 3145732
  8.0 293.0 %all-reduce.2.cloned.1.call-start = ((), (), s32[]{:S(2)}) async-start(), calls=%async_computation.2 | async-start | bytes 524288 | tf_op jit(solution)/shard_map/psum | solution.py:19
  10.0 26.7 %copy-start.2 = (s32[1,1,64,4]{2,3,1,0:T(4,128)S(1)}, s32[1,1,64,4]{2,3,1,0:T(4,128)}, u32[]{:S(2)}) copy-start(s32[1,1,64,4]{2,3,1,0:T(4,128)} %param.15) | copy-start | bytes 3076
  10.0 27.5 %copy-start.1 = (s32[1,1,64]{2,1,0:T(1,128)S(1)}, s32[1,1,64]{2,1,0:T(1,128)}, u32[]{:S(2)}) copy-start(s32[1,1,64]{2,1,0:T(1,128)} %param.16) | copy-start | bytes 772
  10.0 31.0 %collective-permute-start = (bf16[128,256]{1,0:T(8,128)(2,1)S(1)}, bf16[128,256]{1,0:T(8,128)(2,1)S(1)}, u32[]{:S(2)}, u32[]{:S(2)}) collective-permute-start(bf16[128,256]{1,0:T(8,128)(2,1)S(1)} %fusion.2), channel_id=1, source_target_pairs={{0,16},{8,24},{16,32},{24,40},{32,48},{40,56},{48,64},{56,72},{64,... | collective-permute-start | bytes 196616 | tf_op jit(solution)/shard_map/ppermute | solution.py:11
  14.1 26.9 %collective-permute-start.1 = (bf16[128,256]{1,0:T(8,128)(2,1)S(1)}, bf16[128,256]{1,0:T(8,128)(2,1)S(1)}, u32[]{:S(2)}, u32[]{:S(2)}) collective-permute-start(bf16[128,256]{1,0:T(8,128)(2,1)S(1)} %fusion.2), channel_id=1, source_target_pairs={{0,8},{8,16},{16,24},{24,32},{32,40},{40,48},{48,56},{56,64},{64,7... | collective-permute-start | bytes 196616 | tf_op jit(solution)/shard_map/ppermute | solution.py:11
  17.4 23.7 %collective-permute-start.2 = (bf16[128,256]{1,0:T(8,128)(2,1)S(1)}, bf16[128,256]{1,0:T(8,128)(2,1)S(1)}, u32[]{:S(2)}, u32[]{:S(2)}) collective-permute-start(bf16[128,256]{1,0:T(8,128)(2,1)S(1)} %fusion.2), channel_id=1, source_target_pairs={{0,504},{8,0},{16,8},{24,16},{32,24},{40,32},{48,40},{56,48},{64,5... | collective-permute-start | bytes 196616 | tf_op jit(solution)/shard_map/ppermute | solution.py:11
  25.9 15.1 %collective-permute-start.3 = (bf16[128,256]{1,0:T(8,128)(2,1)S(1)}, bf16[128,256]{1,0:T(8,128)(2,1)S(1)}, u32[]{:S(2)}, u32[]{:S(2)}) collective-permute-start(bf16[128,256]{1,0:T(8,128)(2,1)S(1)} %fusion.2), channel_id=1, source_target_pairs={{0,496},{8,504},{16,0},{24,8},{32,16},{40,24},{48,32},{56,40},{64,... | collective-permute-start | bytes 196616 | tf_op jit(solution)/shard_map/ppermute | solution.py:11
  31.2 274.0 %reduce-scatter.2.cloned.1.call-start = ((), (), s32[]{:S(2)}) async-start(), calls=%async_computation.1 | async-start | bytes 1179648 | tf_op jit(solution)/shard_map/reduce_scatter | solution.py:50
Sparse Core Ops, SparseCore 0:
  31.3 269.7 all-reduce.1
Sparse Core Ops, SparseCore 1:
  42.8 41.7 reduce-scatter.1
where the time goes:
time: 315 us; the launch traced here: 314 us
  waiting for transfers between devices  258 us (82%)
  starting transfers between devices  19.4 us (6%)
  between operations  16.4 us (5%)
  other arithmetic  10 us (3%)
  matrix products  7.4 us (2%)
    psum x1, waiting for transfers between devices, on_device(): raw_weight = lax.psum(local_weight, ('blk', 'rep'))  258 us
    ppermute x4, starting transfers between devices, fetched_from(): lax.ppermute(x, axis, [(i, (i - offset) % size) for i in range(size)])  19.3 us
  transfers between devices with their start and end apart: 6, of which 1 were waited for; matrix products, arithmetic and copies ran while one was open for 5% of the time, Pallas kernels for 0%

commit v1 on v0

--- a/solution.py
+++ b/solution.py
@@ -16,7 +16,7 @@
     local_weight = lax.dot_general(
         aggregated, grad_pre, (((0,), (0,)), ((), ())), preferred_element_type=jnp.float32
     )
-    raw_weight = lax.psum(local_weight, ("blk", "rep"))
+    raw_weight = lax.psum(lax.psum(local_weight, "blk"), "rep")
     norm_value = jnp.sqrt(jnp.sum(raw_weight * raw_weight) + 1e-06)
     grad_weight = raw_weight * jnp.minimum(1.0, 128.0 / norm_value)
     inv_root = 1.0 / jnp.sqrt(degree.astype(jnp.float32))

time: 315 us -> 712 us (2.26)
  the two profiles are of different devices: /device:TPU:23 before, /device:TPU:17 now
where the time goes in v1:
time: 712 us
  waiting for transfers between devices  653 us (92%)
  starting transfers between devices  21.3 us (3%)
  between operations  14.6 us (2%)
  other arithmetic  11.1 us (2%)
  matrix products  8.66 us (1%)
    psum x2, waiting for transfers between devices, on_device(): raw_weight = lax.psum(lax.psum(local_weight, 'blk'), 'rep')  613 us
    reduce_scatter x1, waiting for transfers between devices, on_device(): owned = lax.psum_scatter(totals, 'rep', scatter_dimension=0, tiled=True)  40.1 us
    ppermute x4, starting transfers between devices, fetched_from(): lax.ppermute(x, axis, [(i, (i - offset) % size) for i in range(size)])  21.2 us
  transfers between devices with their start and end apart: 7, of which 3 were waited for; matrix products, arithmetic and copies ran while one was open for 3% of the time, Pallas kernels for 0%

profile of v1, /device:TPU:17, one launch (start us, length us, event | category | flops | bytes accessed | tf_op | source)
XLA Modules:
  0.0 711.6 jit_solution(11009445770341718081)
XLA Ops:
  7.2 0.0 copy-start
  7.2 0.0 all-reduce.3.cloned.1.call-start
  7.2 0.7 convert_rsqrt_fusion
  8.0 1.2 fusion.2
  9.1 0.0 copy-start.2
  9.2 0.0 copy-start.1
  9.2 4.1 collective-permute-start
  13.3 3.2 collective-permute-start.1
  16.5 10.5 %collective-permute-start.2 = (bf16[128,256]{1,0:T(8,128)(2,1)S(1)}, bf16[128,256]{1,0:T(8,128)(2,1)S(1)}, u32[]{:S(2)}, u32[]{:S(2)}) collective-permute-start(bf16[128,256]{1,0:T(8,128)(2,1)S(1)} %fusion.2), channel_id=1, source_target_pairs={{0,504},{8,0},{16,8},{24,16},{32,24},{40,32},{48,40},{56,48},{64,5... | collective-permute-start | bytes 196616 | tf_op jit(solution)/shard_map/ppermute | solution.py:11
  27.0 3.4 collective-permute-start.3
  30.4 1.8 convolution_bitcast_fusion.2
  32.2 0.0 all-reduce.3.cloned.1.call-update
  32.2 0.0 all-reduce.5.cloned.1.call-start
  32.3 0.7 compare_and_fusion
  33.0 0.0 copy-done
  33.0 0.6 gather_fusion
  33.6 0.1 broadcast_select_fusion
  33.6 5.2 convert_reduce_fusion
  38.8 0.0 copy-done.2
  38.9 0.1 copy.15
  38.9 0.6 gather_fusion.1
  39.5 0.1 broadcast_select_fusion.1
  39.6 0.0 copy-done.1
  39.6 0.6 gather_fusion.2
  40.2 0.1 iota_compare_fusion.2
  40.3 4.1 convolution_bitcast_fusion
  44.4 0.0 collective-permute-done
  44.4 0.0 collective-permute-done.1
  44.5 0.0 collective-permute-done.2
  44.5 510.8 %all-reduce.3.cloned.1.call-done = f32[256,256]{0,1:T(8,128)} async-done(((f32[256,256]{0,1:T(8,128)}), f32[256,256]{0,1:T(8,128)}) %all-reduce.3.cloned.1.call-update) | async-done | bytes 262160 | tf_op jit(solution)/shard_map/psum | solution.py:19
  555.3 0.0 all-reduce.5.cloned.1.call-update
  555.3 0.0 reduce-scatter.2.cloned.1.call-start
  555.4 0.0 collective-permute-done.3
  555.4 1.6 convolution_bitcast_fusion.1
  557.0 0.0 reduce-scatter.2.cloned.1.call-update
  557.0 102.3 %all-reduce.5.cloned.1.call-done = f32[256,256]{0,1:T(8,128)} async-done(((f32[256,256]{0,1:T(8,128)}), f32[256,256]{0,1:T(8,128)}) %all-reduce.5.cloned.1.call-update) | async-done | bytes 262160 | tf_op jit(solution)/shard_map/psum | solution.py:19
  659.3 1.6 multiply_reduce_fusion
  661.6 1.0 broadcast_multiply_fusion
  662.5 0.8 copy.18
  663.4 40.1 %reduce-scatter.2.cloned.1.call-done = f32[1,128,256]{2,1,0:T(8,128)} async-done(((f32[8,128,256]{2,1,0:T(8,128)}), f32[1,128,256]{2,1,0:T(8,128)}) %reduce-scatter.2.cloned.1.call-update) | async-done | bytes 131088 | tf_op jit(solution)/shard_map/reduce_scatter | solution.py:50
  703.5 1.6 fusion.4
  (7 shorter events, 0.0 us)
Async XLA Ops:
  7.2 25.8 %copy-start = (s32[1,1,64,4,8,128]{5,4,3,2,1,0:T(8,128)S(1)}, s32[1,1,64,4,8,128]{5,4,3,2,1,0:T(8,128)}, u32[]{:S(2)}) copy-start(s32[1,1,64,4,8,128]{5,4,3,2,1,0:T(8,128)} %param.14) | copy-start | bytes 3145732
  7.2 548.1 %all-reduce.3.cloned.1.call-start = ((), (), s32[]{:S(2)}) async-start(), calls=%async_computation.2 | async-start | bytes 524288 | tf_op jit(solution)/shard_map/psum | solution.py:19
  9.1 29.7 %copy-start.2 = (s32[1,1,64,4]{2,3,1,0:T(4,128)S(1)}, s32[1,1,64,4]{2,3,1,0:T(4,128)}, u32[]{:S(2)}) copy-start(s32[1,1,64,4]{2,3,1,0:T(4,128)} %param.15) | copy-start | bytes 3076
  9.2 30.4 %copy-start.1 = (s32[1,1,64]{2,1,0:T(1,128)S(1)}, s32[1,1,64]{2,1,0:T(1,128)}, u32[]{:S(2)}) copy-start(s32[1,1,64]{2,1,0:T(1,128)} %param.16) | copy-start | bytes 772
  9.2 35.2 %collective-permute-start = (bf16[128,256]{1,0:T(8,128)(2,1)S(1)}, bf16[128,256]{1,0:T(8,128)(2,1)S(1)}, u32[]{:S(2)}, u32[]{:S(2)}) collective-permute-start(bf16[128,256]{1,0:T(8,128)(2,1)S(1)} %fusion.2), channel_id=1, source_target_pairs={{0,16},{8,24},{16,32},{24,40},{32,48},{40,56},{48,64},{56,72},{64,... | collective-permute-start | bytes 196616 | tf_op jit(solution)/shard_map/ppermute | solution.py:11
  13.3 31.1 %collective-permute-start.1 = (bf16[128,256]{1,0:T(8,128)(2,1)S(1)}, bf16[128,256]{1,0:T(8,128)(2,1)S(1)}, u32[]{:S(2)}, u32[]{:S(2)}) collective-permute-start(bf16[128,256]{1,0:T(8,128)(2,1)S(1)} %fusion.2), channel_id=1, source_target_pairs={{0,8},{8,16},{16,24},{24,32},{32,40},{40,48},{48,56},{56,64},{64,7... | collective-permute-start | bytes 196616 | tf_op jit(solution)/shard_map/ppermute | solution.py:11
  16.5 27.9 %collective-permute-start.2 = (bf16[128,256]{1,0:T(8,128)(2,1)S(1)}, bf16[128,256]{1,0:T(8,128)(2,1)S(1)}, u32[]{:S(2)}, u32[]{:S(2)}) collective-permute-start(bf16[128,256]{1,0:T(8,128)(2,1)S(1)} %fusion.2), channel_id=1, source_target_pairs={{0,504},{8,0},{16,8},{24,16},{32,24},{40,32},{48,40},{56,48},{64,5... | collective-permute-start | bytes 196616 | tf_op jit(solution)/shard_map/ppermute | solution.py:11
  27.0 528.3 %collective-permute-start.3 = (bf16[128,256]{1,0:T(8,128)(2,1)S(1)}, bf16[128,256]{1,0:T(8,128)(2,1)S(1)}, u32[]{:S(2)}, u32[]{:S(2)}) collective-permute-start(bf16[128,256]{1,0:T(8,128)(2,1)S(1)} %fusion.2), channel_id=1, source_target_pairs={{0,496},{8,504},{16,0},{24,8},{32,16},{40,24},{48,32},{56,40},{64,... | collective-permute-start | bytes 196616 | tf_op jit(solution)/shard_map/ppermute | solution.py:11
  32.2 627.0 %all-reduce.5.cloned.1.call-start = ((), (), s32[]{:S(2)}) async-start(), calls=%async_computation.3 | async-start | bytes 524288 | tf_op jit(solution)/shard_map/psum | solution.py:19
  555.3 148.1 %reduce-scatter.2.cloned.1.call-start = ((), (), s32[]{:S(2)}) async-start(), calls=%async_computation.1 | async-start | bytes 1179648 | tf_op jit(solution)/shard_map/reduce_scatter | solution.py:50
Sparse Core Ops, SparseCore 0:
  32.4 522.8 all-reduce.2
  558.5 100.7 all-reduce.4
  662.1 41.3 reduce-scatter.1
